TPU v7x, 512 devices: a whole 4x8x8 slice. The times are simulated.
512 devices in a mesh: seq: 16 (over z, core), expert: 32 (over x, y).
Axes of the slice: x: 4, y: 8, z: 8, core: 2. Of those that a mesh axis runs over, the one named last changes fastest.
Arguments:
- hidden: bfloat16 [32, 1024, 2048], P('expert', 'seq'), may hold values from -6 to 6
- queries: bfloat16 [32, 1024, 4608], P('expert', 'seq'), may hold values from -5 to 5
- suffix_latent: bfloat16 [32, 1024, 576], P('expert', 'seq'), may hold values from -6 to 6
- prefix_latent: bfloat16 [2, 1024, 576], P(None, 'seq'), may hold values from -6 to 6
- lengths: int32 [32, 4], P('expert'), may hold values from 1 to 512, 1024 in all within a row
- prefix_of: int32 [32, 4], P('expert'), may hold values from 0 to 1
- value_up: bfloat16 [8, 512, 128], replicated, may hold values from -1 to 1
- out_proj: bfloat16 [1024, 2048], P(None, 'expert'), may hold values from -0.1875 to 0.1875
- norm_gain: float32 [2048], replicated, may hold values from 0.5 to 1.5
- router: bfloat16 [2048, 32], replicated, may hold values from -0.0625 to 0.0625
- routes: int32 [32, 1024, 6], P('expert', 'seq'), may hold values from 0 to 31, all different within a row; in each aligned block of 64 rows (0 to 63, 64 to 127, ..., all dimensions but the last counted through in order) at most 16 rows name the same one
- expert_in: bfloat16 [32, 2048, 1408], P('expert', 'seq'), may hold values from -0.125 to 0.125
- expert_out: bfloat16 [32, 2048, 704], P('expert', 'seq'), may hold values from -1.25 to 1.25
Outputs:
- layer_out: bfloat16 [32, 1024, 2048], P('expert', 'seq')
Inputs may be any that keep to these rules, and one draw needn't show every extreme that they name: `routes`: among the rows of one device (aligned blocks of 64 tokens) no expert is named more than 16 times, a bound that some block reaches; a token's 6 experts differ. `lengths`: each row sums to 1024; its longest request has exactly 512 tokens.
All inputs are finite; a program needn't handle non-finite values.
Results may differ from a plain program's by a relative error of at most 0.013.
Values may be sent and summed in bfloat16 or wider, within the bound.
No kernel may reach another device: no remote copies, remote signals or barrier semaphores. Data moves between devices by JAX's collectives and lax.ppermute only.
A program may use at most 128 MiB of HBM per device.

v0:
```python
import jax
import jax.numpy as jnp
from jax import lax
from jax.sharding import PartitionSpec as P

qk_scale = 192.0 ** (-0.5)
big_negative = -1e30


def request_of(positions, request_ends):
    return jnp.sum((positions[:, None] >= request_ends[None, :]).astype(jnp.int32), axis=1)


def merge_scores(running, scores, allowed, values):
    running_max, running_sum, running_acc = running
    new_max = jnp.maximum(running_max, jnp.max(jnp.where(allowed, scores, big_negative), axis=2))
    weights = jnp.where(allowed, jnp.exp(scores - new_max[:, :, None]), 0.0)
    new_sum = jnp.sum(weights, axis=2)
    new_acc = jnp.einsum(
        "thn,nl->thl", weights.astype(jnp.bfloat16), values, preferred_element_type=jnp.float32
    )
    return (new_max, new_sum, new_acc)


def local(
    hidden,
    queries,
    suffix_latent,
    prefix_latent,
    lengths,
    prefix_of,
    value_up,
    out_proj,
    norm_gain,
    router,
    routes,
    expert_in,
    expert_out,
):
    local_tokens = hidden.shape[1]
    model_width = hidden.shape[2]
    key_width = suffix_latent.shape[2]
    head_count = value_up.shape[0]
    latent_width = value_up.shape[1]
    expert_count = router.shape[1]
    top_count = routes.shape[2]
    capacity = 4 * local_tokens * top_count // (3 * expert_count)
    request_count = lengths.shape[1]
    request_ends = jnp.cumsum(lengths[0])
    my_positions = lax.axis_index("seq") * local_tokens + jnp.arange(local_tokens, dtype=jnp.int32)
    my_requests = request_of(my_positions, request_ends)
    request_ids = jnp.arange(request_count, dtype=jnp.int32)
    chosen = jnp.sum(
        jnp.where(my_requests[:, None] == request_ids[None, :], prefix_of[0][None, :], 0), axis=1
    )
    prefix_pick = chosen[:, None] == jnp.arange(2, dtype=jnp.int32)[None, :]
    single_prefix = jnp.all(chosen == chosen[0])
    my_prefix = chosen[0]
    query_rows = queries[0].reshape(local_tokens, head_count, key_width)
    start_state = (
        jnp.full((local_tokens, head_count), big_negative, jnp.float32),
        jnp.zeros((local_tokens, head_count), jnp.float32),
        jnp.zeros((local_tokens, head_count, latent_width), jnp.float32),
    )
    suffix_piece = lax.all_gather(suffix_latent, "seq", axis=1, tiled=True)
    prefix_piece = lax.all_gather(prefix_latent, "seq", axis=1, tiled=True)
    piece_rows = suffix_piece.shape[1]
    suffix_keys = suffix_piece[0]
    key_positions = jnp.arange(piece_rows, dtype=jnp.int32)
    key_requests = request_of(key_positions, request_ends)
    suffix_allowed = (key_requests[None, :] == my_requests[:, None]) & (
        key_positions[None, :] <= my_positions[:, None]
    )
    suffix_scores = (
        jnp.einsum("thk,nk->thn", query_rows, suffix_keys, preferred_element_type=jnp.float32)
        * qk_scale
    )

    def one_prefix(running_state):
        chosen_keys = lax.dynamic_index_in_dim(prefix_piece, my_prefix, 0, keepdims=False)
        prefix_scores = (
            jnp.einsum("thk,nk->thn", query_rows, chosen_keys, preferred_element_type=jnp.float32)
            * qk_scale
        )
        scores = jnp.concatenate([suffix_scores, prefix_scores], axis=2)
        every_key = jnp.ones((local_tokens, piece_rows), dtype=bool)
        allowed = jnp.concatenate([suffix_allowed, every_key], axis=1)[:, None, :]
        values = jnp.concatenate(
            [suffix_keys[:, :latent_width], chosen_keys[:, :latent_width]], axis=0
        )
        return merge_scores(running_state, scores, allowed, values)

    def two_prefixes(running_state):
        prefix_scores = (
            jnp.einsum(
                "thk,pnk->thpn", query_rows, prefix_piece, preferred_element_type=jnp.float32
            )
            * qk_scale
        )
        scores = jnp.concatenate(
            [suffix_scores, prefix_scores.reshape(local_tokens, head_count, 2 * piece_rows)], axis=2
        )
        prefix_allowed = jnp.broadcast_to(
            prefix_pick[:, :, None], (local_tokens, 2, piece_rows)
        ).reshape(local_tokens, 2 * piece_rows)
        allowed = jnp.concatenate([suffix_allowed, prefix_allowed], axis=1)[:, None, :]
        values = jnp.concatenate(
            [
                suffix_keys[:, :latent_width],
                prefix_piece[:, :, :latent_width].reshape(2 * piece_rows, latent_width),
            ],
            axis=0,
        )
        return merge_scores(running_state, scores, allowed, values)

    final_max, final_sum, final_acc = lax.cond(single_prefix, one_prefix, two_prefixes, start_state)
    latent_out = (final_acc / final_sum[:, :, None]).astype(jnp.bfloat16)
    value_out = jnp.einsum(
        "thl,hlv->thv", latent_out, value_up, preferred_element_type=jnp.float32
    ).astype(jnp.bfloat16)
    value_out = value_out.reshape(local_tokens, head_count * value_up.shape[2])
    projected = jnp.dot(
        value_out,
        lax.all_gather(out_proj, "expert", axis=1, tiled=True),
        preferred_element_type=jnp.float32,
    )
    residual = hidden[0].astype(jnp.float32) + projected
    normed = (
        residual
        * lax.rsqrt(jnp.mean(residual * residual, axis=1, keepdims=True) + 1e-06)
        * norm_gain
    ).astype(jnp.bfloat16)
    logits = jnp.dot(normed, router, preferred_element_type=jnp.float32)
    expert_probs = jax.nn.softmax(logits, axis=1)
    expert_ids = jnp.arange(expert_count, dtype=jnp.int32)
    my_routes = routes[0]
    matches = my_routes[:, :, None] == expert_ids[None, None, :]
    gate_values = jnp.sum(jnp.where(matches, expert_probs[:, None, :], 0.0), axis=2)
    flat_hits = matches.reshape(local_tokens * top_count, expert_count).astype(jnp.int32)
    earlier = jnp.cumsum(flat_hits, axis=0) - flat_hits
    slot_index = jnp.sum(earlier * flat_hits, axis=1).reshape(local_tokens, top_count)
    cell_index = my_routes * capacity + slot_index
    cell_ids = jnp.arange(expert_count * capacity, dtype=jnp.int32)
    placing = jnp.sum(
        (cell_ids[:, None, None] == cell_index[None, :, :]).astype(jnp.int32), axis=2
    ).astype(jnp.bfloat16)
    outgoing = jnp.dot(placing, normed, preferred_element_type=jnp.float32).astype(jnp.bfloat16)
    outgoing = outgoing.reshape(expert_count, capacity, model_width)
    incoming = lax.all_to_all(outgoing, "expert", split_axis=0, concat_axis=0, tiled=True)
    full_in, full_out = (
        lax.all_gather(expert_in, "seq", axis=1, tiled=True),
        lax.all_gather(expert_out, "seq", axis=1, tiled=True),
    )
    all_rows = incoming.reshape(-1, model_width)
    gate_up = jnp.dot(all_rows, full_in[0], preferred_element_type=jnp.float32)
    hidden_units = gate_up.shape[1] // 2
    active = (jax.nn.silu(gate_up[:, :hidden_units]) * gate_up[:, hidden_units:]).astype(
        jnp.bfloat16
    )
    produced = lax.dot_general(
        active, full_out[0], (((1,), (1,)), ((), ())), preferred_element_type=jnp.float32
    ).astype(jnp.bfloat16)
    returned = lax.all_to_all(
        produced.reshape(-1, capacity, model_width),
        "expert",
        split_axis=0,
        concat_axis=0,
        tiled=True,
    )
    returned_rows = returned.reshape(-1, model_width)
    picked = returned_rows[cell_index]
    routed_sum = jnp.sum(gate_values[:, :, None] * picked.astype(jnp.float32), axis=1)
    layer_out = (residual + routed_sum).astype(jnp.bfloat16)
    return layer_out[None]


def solution(mesh):
    in_specs = (
        P("expert", "seq", None),
        P("expert", "seq", None),
        P("expert", "seq", None),
        P(None, "seq", None),
        P("expert", None),
        P("expert", None),
        P(),
        P(None, "expert"),
        P(),
        P(),
        P("expert", "seq", None),
        P("expert", "seq", None),
        P("expert", "seq", None),
    )
    out_specs = P("expert", "seq", None)
    return jax.shard_map(local, mesh=mesh, in_specs=in_specs, out_specs=out_specs, check_vma=False)
```

profile of v0, /device:TPU:16, one launch (start us, length us, event | category | flops | bytes accessed | tf_op | source)
XLA Modules:
  0.0 368.0 jit_solution(16596417180253832410)
XLA Ops:
  6.5 0.7 all-gather.8.cloned.1.call-update
  7.3 1.8 copy.86
  9.1 0.7 all-gather.10.cloned.1.call-update
  9.9 0.5 all-gather.12.cloned.1.call-update
  10.4 0.5 all-gather.14.cloned.1.call-update
  11.0 0.8 copy.97
  12.1 0.8 reduce-window.18
  13.2 0.7 select_reduce_fusion.3
  13.9 2.4 reshape_squeeze.3
  16.4 0.7 compare_reduce_fusion
  17.7 0.9 reduce-window.19
  18.6 0.2 slice_reduce_fusion
  19.2 0.8 convert_reduce_fusion
  20.0 36.3 %all-gather.8.cloned.1.call-done = bf16[1,1024,576]{2,1,0:T(8,128)(2,1)} async-done(((bf16[1,64,576]{2,1,0:T(8,128)(2,1)}), bf16[1,1024,576]{2,1,0:T(8,128)(2,1)}) %all-gather.8.cloned.1.call-update) | async-done | bytes 1179664 | tf_op jit(solution)/shard_map/all_gather | solution.py:65
  56.3 2.4 copy.87
  58.7 2.5 convolution_multiply_fusion
  61.3 39.0 %all-gather.6.cloned.1.call-done = bf16[2,1024,576]{2,0,1:T(2,128)(2,1)} async-done(((bf16[2,64,576]{2,0,1:T(2,128)(2,1)}), bf16[2,1024,576]{2,0,1:T(2,128)(2,1)}) %all-gather.6.cloned.1.call-update) | async-done | bytes 2359312 | tf_op jit(solution)/shard_map/all_gather | solution.py:66
  100.3 31.3 %conditional.1 = (f32[64,8,512]{2,1,0:T(8,128)}, f32[64,8]{1,0:T(8,128)S(1)}) conditional(s32[]{:T(128)} %convert_element_type.64, (s32[64]{0:T(128)S(1)}, s32[64,2]{1,0:T(8,128)S(1)}, pred[64,1024]{1,0:T(8,128)(4,1)S(1)}, bf16[64,8,576]{2,1,0:T(8,128)(2,1)}, bf16[2,1024,576]{2,0,1:T(2,128)(2,1)}, /*index=5*/f32[64,8,1024]{2,1,0:T(8,128)S(1)}, ...), branch_computations={%region_5.8_spmd, %region_8.11_spmd} | conditional | flops 2843409920 | bytes 92157032 | solution.py:116
  100.3 7.4 %copy.88 = bf16[2,1024,576]{1,2,0:T(8,128)(2,1)} copy(bf16[2,1024,576]{2,0,1:T(2,128)(2,1)} %get-tuple-element.110) | data formatting | bytes 4718592 | tf_op jit(solution)/shard_map
  107.6 3.7 fusion.10
  111.7 1.2 select_reduce_fusion
  112.9 0.5 copy-done.1
  113.4 1.1 copy-done.4
  114.5 1.5 slice.36
  116.0 4.0 %copy.82 = bf16[2,1024,512]{2,1,0:T(8,128)(2,1)} copy(bf16[2,1024,512]{1,2,0:T(8,128)(2,1)} %slice.36) | data formatting | bytes 4194304 | tf_op jit(solution)/shard_map/cond/branch_0_fun/slice | solution.py:110
  120.0 2.4 copy.89
  122.4 1.3 slice.35
  123.7 5.9 %fusion.2 = f32[64,8,512]{2,1,0:T(8,128)} fusion(bf16[2048,512]{1,0:T(8,128)(2,1)} %bitcast.104, bf16[1024,512]{1,0:T(8,128)(2,1)S(1)} %slice.35, f32[64,8,2048]{2,1,0:T(8,128)} %bitcast.98, f32[64,8,1024]{2,1,0:T(8,128)S(1)} %get-tuple-element.36, f32[64,8]{1,0:T(8,128)S(1)} %broadcast_maximum_fusion, pred[64,3072]{1,0:T(8,128)(4,1)S(1)} %pad_add_fusion), kind=kOutput, calls=%fused_computation.7 | convolution fusion | flops 1623195648 | bytes 10684416 | tf_op jit(solution)/shard_map/cond/branch_0_fun/thn,nl->thl/dot_general | solution.py:19
  129.6 1.8 fusion.1
  131.5 1.4 divide_convert_fusion
  133.0 0.4 fusion.33
  133.4 54.2 %all-gather.10.cloned.1.call-done = bf16[1024,2048]{0,1:T(8,128)(2,1)} async-done(((bf16[1024,64]{0,1:T(8,128)(2,1)}), bf16[1024,2048]{0,1:T(8,128)(2,1)}) %all-gather.10.cloned.1.call-update) | async-done | bytes 4194320 | tf_op jit(solution)/shard_map/all_gather | solution.py:124
  187.6 3.7 %multiply_reduce_fusion.1 = (f32[64]{0:T(128)S(1)}, f32[64,2048]{1,0:T(8,128)S(1)}) fusion(bf16[1024,2048]{0,1:T(8,128)(2,1)} %all-gather.10.cloned.1.call-done, bf16[8,8,8,128]{3,2,1,0:T(8,128)(2,1)S(1)} %fusion.33, bf16[1,64,2048]{2,1,0:T(8,128)(2,1)S(1)} %copy-done.9), kind=kOutput, calls=%fused_computation.60 | convolution fusion | flops 268959680 | bytes 5112064 | tf_op jit(solution)/shard_map/dot_general | solution.py:122
  191.3 0.8 copy-done.5
  192.1 2.1 convolution_convert_fusion.1
  194.1 7.2 %all-to-all-start = ((bf16[32,16,2048]{2,1,0:T(8,128)(2,1)}), bf16[32,16,2048]{2,1,0:T(8,128)(2,1)S(1)}, u32[]{:S(2)}, u32[]{:S(2)}) async-start(bf16[32,16,2048]{2,1,0:T(8,128)(2,1)} %bitcast.20), calls=%async_computation | async-start | bytes 4194304 | tf_op jit(solution)/shard_map/all_to_all | solution.py:149
  201.3 34.9 %all-gather.12.cloned.1.call-done = bf16[1,2048,1408]{2,1,0:T(8,128)(2,1)} async-done(((bf16[1,128,1408]{2,1,0:T(8,128)(2,1)}), bf16[1,2048,1408]{2,1,0:T(8,128)(2,1)}) %all-gather.12.cloned.1.call-update) | async-done | bytes 5767184 | tf_op jit(solution)/shard_map/all_gather | solution.py:151
  236.2 11.3 %all-to-all-done = bf16[32,16,2048]{2,1,0:T(8,128)(2,1)S(1)} async-done(((bf16[32,16,2048]{2,1,0:T(8,128)(2,1)}), bf16[32,16,2048]{2,1,0:T(8,128)(2,1)S(1)}, u32[]{:S(2)}, u32[]{:S(2)}) %all-to-all-start) | async-done | bytes 2097184 | tf_op jit(solution)/shard_map/all_to_all | solution.py:149
  247.5 7.6 %fusion.28 = f32[512,1408]{1,0:T(8,128)} fusion(bf16[512,2048]{1,0:T(8,128)(2,1)S(1)} %bitcast.103, bf16[1,2048,1408]{2,1,0:T(8,128)(2,1)} %all-gather.12.cloned.1.call-done), kind=kOutput, calls=%fused_computation.40 | convolution fusion | flops 2952790016 | bytes 10747904 | tf_op jit(solution)/shard_map/dot_general | solution.py:155
  255.2 28.3 %all-gather.14.cloned.1.call-done = bf16[1,2048,704]{1,2,0:T(8,128)(2,1)} async-done(((bf16[1,128,704]{1,2,0:T(8,128)(2,1)}), bf16[1,2048,704]{1,2,0:T(8,128)(2,1)}) %all-gather.14.cloned.1.call-update) | async-done | bytes 2883600 | tf_op jit(solution)/shard_map/all_gather | solution.py:152
  283.5 6.0 %convolution_convert_fusion = bf16[512,2048]{1,0:T(8,128)(2,1)} fusion(bf16[1,2048,704]{1,2,0:T(8,128)(2,1)} %all-gather.14.cloned.1.call-done, f32[512,1408]{1,0:T(8,128)} %fusion.28), kind=kOutput, calls=%fused_computation.43 | convolution fusion | flops 1479606272 | bytes 8126464 | tf_op jit(solution)/shard_map/dot_general | solution.py:160
  289.5 10.0 %all-to-all-start.1 = ((bf16[32,16,2048]{2,1,0:T(8,128)(2,1)}), bf16[32,16,2048]{2,1,0:T(8,128)(2,1)S(1)}, u32[]{:S(2)}, u32[]{:S(2)}) async-start(bf16[32,16,2048]{2,1,0:T(8,128)(2,1)} %bitcast.102), calls=%async_computation.1 | async-start | bytes 4194304 | tf_op jit(solution)/shard_map/all_to_all | solution.py:163
  299.8 1.3 fusion.50
  301.3 48.6 %all-to-all-done.1 = bf16[32,16,2048]{2,1,0:T(8,128)(2,1)S(1)} async-done(((bf16[32,16,2048]{2,1,0:T(8,128)(2,1)}), bf16[32,16,2048]{2,1,0:T(8,128)(2,1)S(1)}, u32[]{:S(2)}, u32[]{:S(2)}) %all-to-all-start.1) | async-done | bytes 2097184 | tf_op jit(solution)/shard_map/all_to_all | solution.py:163
  349.9 3.1 gather_fusion
  353.0 3.9 %reshape.155 = f32[64,6,2048]{2,1,0:T(8,128)} reshape(bf16[384,2048]{1,0:T(8,128)(2,1)} %gather_fusion) | data formatting | bytes 4718592 | tf_op jit(solution)/shard_map/convert_element_type | solution.py:172
  356.9 3.8 %multiply_reduce_fusion = f32[64,2048]{1,0:T(8,128)S(1)} fusion(f32[64,6,2048]{2,1,0:T(8,128)} %reshape.155, f32[64,6]{1,0:T(8,128)S(1)} %copy.96), kind=kLoop, calls=%fused_computation.42 | loop fusion | flops 1441792 | bytes 3671552 | tf_op jit(solution)/shard_map/reduce_sum | solution.py:172
  360.7 0.8 fusion.37
  (53 shorter events, 2.0 us)
Async XLA Ops:
  6.5 126.4 %copy-start = (bf16[8,512,128]{2,1,0:T(8,128)(2,1)S(1)}, bf16[8,512,128]{2,1,0:T(8,128)(2,1)}, u32[]{:S(2)}) copy-start(bf16[8,512,128]{2,1,0:T(8,128)(2,1)} %param.21) | copy-start | bytes 3145732
  6.5 49.8 %all-gather.8.cloned.1.call-start = ((), (), s32[]{:S(2)}) async-start(), calls=%async_computation.3 | async-start | bytes 1392640 | tf_op jit(solution)/shard_map/all_gather | solution.py:65
  7.3 93.0 %all-gather.6.cloned.1.call-start = ((), (), s32[]{:S(2)}) async-start(), calls=%async_computation.2 | async-start | bytes 2785280 | tf_op jit(solution)/shard_map/all_gather | solution.py:66
  9.1 178.5 %all-gather.10.cloned.1.call-start = ((), (), s32[]{:S(2)}) async-start(), calls=%async_computation.4 | async-start | bytes 4325376 | tf_op jit(solution)/shard_map/all_gather | solution.py:124
  9.8 226.4 %all-gather.12.cloned.1.call-start = ((), (), s32[]{:S(2)}) async-start(), calls=%async_computation.5 | async-start | bytes 6127616 | tf_op jit(solution)/shard_map/all_gather | solution.py:151
  10.4 273.1 %all-gather.14.cloned.1.call-start = ((), (), s32[]{:S(2)}) async-start(), calls=%async_computation.6 | async-start | bytes 3063808 | tf_op jit(solution)/shard_map/all_gather | solution.py:152
  111.3 2.1 copy-start.1
  111.7 2.7 copy-start.4
  123.7 5.9 %copy-start.2 = (f32[64,8,2,1024]{3,1,2,0:T(8,128)S(1)}, f32[64,8,2,1024]{3,1,2,0:T(8,128)}, u32[]{:S(2)}) copy-start(f32[64,8,2,1024]{3,1,2,0:T(8,128)} %copy-done.1) | copy-start | bytes 12582916 | tf_op jit(solution)/shard_map/cond
  131.5 56.0 %copy-start.9 = (bf16[1,64,2048]{2,1,0:T(8,128)(2,1)S(1)}, bf16[1,64,2048]{2,1,0:T(8,128)(2,1)}, u32[]{:S(2)}) copy-start(bf16[1,64,2048]{2,1,0:T(8,128)(2,1)} %param.15) | copy-start | bytes 786436
  133.3 58.7 %copy-start.8 = (s32[512,64]{0,1:T(8,128)S(1)}, s32[512,64]{0,1:T(8,128)}, u32[]{:S(2)}) copy-start(s32[512,64]{0,1:T(8,128)} %convert_reduce_fusion) | copy-start | bytes 393220
  133.3 58.7 %copy-start.11 = (f32[2048]{0:T(1024)S(1)}, f32[2048]{0:T(1024)}, u32[]{:S(2)}) copy-start(f32[2048]{0:T(1024)} %param.23) | copy-start | bytes 24580
  191.2 0.8 copy-start.5
  194.1 53.4 %all-to-all-start = ((bf16[32,16,2048]{2,1,0:T(8,128)(2,1)}), bf16[32,16,2048]{2,1,0:T(8,128)(2,1)S(1)}, u32[]{:S(2)}, u32[]{:S(2)}) async-start(bf16[32,16,2048]{2,1,0:T(8,128)(2,1)} %bitcast.20), calls=%async_computation | async-start | bytes 4194304 | tf_op jit(solution)/shard_map/all_to_all | solution.py:149
  289.5 10.0 %copy-start.12 = (s32[1,64,6]{1,0,2:T(1,128)S(1)}, s32[1,64,6]{1,0,2:T(1,128)}, u32[]{:S(2)}) copy-start(s32[1,64,6]{1,0,2:T(1,128)} %param.25) | copy-start | bytes 4612
  289.5 10.3 %copy-start.10 = (bf16[2048,32]{0,1:T(8,128)(2,1)S(1)}, bf16[2048,32]{0,1:T(8,128)(2,1)}, u32[]{:S(2)}) copy-start(bf16[2048,32]{0,1:T(8,128)(2,1)} %param.24) | copy-start | bytes 393220
  289.5 60.4 %all-to-all-start.1 = ((bf16[32,16,2048]{2,1,0:T(8,128)(2,1)}), bf16[32,16,2048]{2,1,0:T(8,128)(2,1)S(1)}, u32[]{:S(2)}, u32[]{:S(2)}) async-start(bf16[32,16,2048]{2,1,0:T(8,128)(2,1)} %bitcast.102), calls=%async_computation.1 | async-start | bytes 4194304 | tf_op jit(solution)/shard_map/all_to_all | solution.py:163
  356.9 3.8 %copy-start.6 = (f32[64,2048]{1,0:T(8,128)S(1)}, f32[64,2048]{1,0:T(8,128)}, u32[]{:S(2)}) copy-start(f32[64,2048]{1,0:T(8,128)} %copy-done.5) | copy-start | bytes 1572868
Sparse Core Ops, SparseCore 0:
  9.5 46.7 all-gather.7
  58.4 41.7 all-gather.5
  103.4 84.0 all-gather.9
  189.5 46.6 all-gather.11
  238.1 45.3 all-gather.13
where the time goes:
time: 369 us; the launch traced here: 368 us
  waiting for transfers between devices  255 us (69%)
  local copies, waits for them, and re-layouts  34.7 us (9%)
  matrix products  33.2 us (9%)
  starting transfers between devices  17.3 us (5%)
  between operations  14 us (4%)
  other arithmetic  13.5 us (4%)
    all_gather x1, waiting for transfers between devices, local(): lax.all_gather(out_proj, 'expert', axis=1, tiled=True)  54.2 us
    all_to_all x1, waiting for transfers between devices, local(): lax.all_to_all(produced.reshape(-1, capacity, model_width), 'expert', spl...  48.6 us
    all_gather x1, waiting for transfers between devices, local(): prefix_piece = lax.all_gather(prefix_latent, 'seq', axis=1, tiled=True)  39 us
    all_gather x1, waiting for transfers between devices, local(): suffix_piece = lax.all_gather(suffix_latent, 'seq', axis=1, tiled=True)  36.3 us
    all_gather x1, waiting for transfers between devices, local(): lax.all_gather(expert_in, 'seq', axis=1, tiled=True)  34.9 us
    all_gather x1, waiting for transfers between devices, local(): lax.all_gather(expert_out, 'seq', axis=1, tiled=True)  28.3 us
    all_to_all x1, waiting for transfers between devices, local(): lax.all_to_all(outgoing, 'expert', split_axis=0, concat_axis=0, tiled=True)  11.3 us
    all_to_all x1, starting transfers between devices, local(): lax.all_to_all(produced.reshape(-1, capacity, model_width), 'expert', spl...  9.96 us
  transfers between devices with their start and end apart: 7, of which 7 were waited for; matrix products, arithmetic and copies ran while one was open for 17% of the time, Pallas kernels for 0%

commit v1 on v0

--- a/solution.py
+++ b/solution.py
@@ -5,6 +5,19 @@
 
 qk_scale = 192.0 ** (-0.5)
 big_negative = -1e30
+
+
+def collect(array, axis, dim):
+    ways = lax.axis_size(axis)
+    up = [(d, (d + 1) % ways) for d in range(ways)]
+    down = [(d, (d - 1) % ways) for d in range(ways)]
+    earlier, later = ([array], [array])
+    for _ in range(ways // 2):
+        earlier.append(lax.ppermute(earlier[-1], axis, up))
+    for _ in range((ways - 1) // 2):
+        later.append(lax.ppermute(later[-1], axis, down))
+    line = jnp.concatenate([*earlier[::-1], *later[1:]], axis=dim)
+    return jnp.roll(line, (lax.axis_index(axis) - ways // 2) * array.shape[dim], axis=dim)
 
 
 def request_of(positions, request_ends):
@@ -149,7 +162,7 @@
     incoming = lax.all_to_all(outgoing, "expert", split_axis=0, concat_axis=0, tiled=True)
     full_in, full_out = (
         lax.all_gather(expert_in, "seq", axis=1, tiled=True),
-        lax.all_gather(expert_out, "seq", axis=1, tiled=True),
+        collect(expert_out, "seq", 1),
     )
     all_rows = incoming.reshape(-1, model_width)
     gate_up = jnp.dot(all_rows, full_in[0], preferred_element_type=jnp.float32)

time: 369 us -> 342 us (0.927)
  the two profiles are of different devices: /device:TPU:16 before, /device:TPU:8 now
where the time goes in v1:
time: 342 us; the launch traced here: 341 us
  waiting for transfers between devices  180 us (53%)
  local copies, waits for them, and re-layouts  69.2 us (20%)
  starting transfers between devices  40.6 us (12%)
  matrix products  24.5 us (7%)
  between operations  14.2 us (4%)
  other arithmetic  12.6 us (4%)
    all_gather x1, waiting for transfers between devices, local(): lax.all_gather(out_proj, 'expert', axis=1, tiled=True)  69 us
    all_to_all x1, waiting for transfers between devices, local(): lax.all_to_all(produced.reshape(-1, capacity, model_width), 'expert', spl...  46.8 us
    unnamed x78, local copies, waits for them, and re-layouts  43.1 us
    all_gather x1, waiting for transfers between devices, local(): prefix_piece = lax.all_gather(prefix_latent, 'seq', axis=1, tiled=True)  37.3 us
    ppermute x7, starting transfers between devices, collect(): later.append(lax.ppermute(later[-1], axis, down))  24.2 us
    ppermute x8, waiting for transfers between devices, collect(): earlier.append(lax.ppermute(earlier[-1], axis, up))  19 us
    all_to_all x1, starting transfers between devices, local(): lax.all_to_all(produced.reshape(-1, capacity, model_width), 'expert', spl...  9.86 us
    another operation x2, local copies, waits for them, and re-layouts  8.56 us
  transfers between devices with their start and end apart: 21, of which 10 were waited for; matrix products, arithmetic and copies ran while one was open for 24% of the time, Pallas kernels for 0%

profile of v1, /device:TPU:8, one launch (start us, length us, event | category | flops | bytes accessed | tf_op | source)
XLA Modules:
  0.0 341.0 jit_solution(7662982555751663368)
XLA Ops:
  7.3 1.7 copy.86
  10.4 8.5 %collective-permute-start.8 = (bf16[1,128,704]{1,2,0:T(8,128)(2,1)}, bf16[1,128,704]{1,2,0:T(8,128)(2,1)S(1)}, u32[]{:S(2)}, u32[]{:S(2)}) collective-permute-start(bf16[1,128,704]{1,2,0:T(8,128)(2,1)} %param.27), channel_id=1, source_target_pairs={{0,480},{32,0},{64,32},{96,64},{128,96},{160,128},{192,160},{224,1... | collective-permute-start | bytes 540680 | tf_op jit(solution)/shard_map/ppermute | solution.py:18
  22.9 2.4 reshape_squeeze.3
  26.2 5.2 %collective-permute-done.1 = bf16[1,128,704]{1,2,0:T(8,128)(2,1)S(1)} collective-permute-done((bf16[1,128,704]{1,2,0:T(8,128)(2,1)S(1)}, bf16[1,128,704]{1,2,0:T(8,128)(2,1)S(1)}, u32[]{:S(2)}, u32[]{:S(2)}) %collective-permute-start.1) | collective-permute-done | bytes 180256 | tf_op jit(solution)/shard_map/ppermute | solution.py:16
  32.0 3.0 collective-permute-start.9
  34.9 3.5 %collective-permute-done.2 = bf16[1,128,704]{1,2,0:T(8,128)(2,1)S(1)} collective-permute-done((bf16[1,128,704]{1,2,0:T(8,128)(2,1)S(1)}, bf16[1,128,704]{1,2,0:T(8,128)(2,1)S(1)}, u32[]{:S(2)}, u32[]{:S(2)}) %collective-permute-start.2) | collective-permute-done | bytes 180256 | tf_op jit(solution)/shard_map/ppermute | solution.py:16
  38.5 3.4 collective-permute-start.10
  41.9 3.5 %collective-permute-done.3 = bf16[1,128,704]{1,2,0:T(8,128)(2,1)S(1)} collective-permute-done((bf16[1,128,704]{1,2,0:T(8,128)(2,1)S(1)}, bf16[1,128,704]{1,2,0:T(8,128)(2,1)S(1)}, u32[]{:S(2)}, u32[]{:S(2)}) %collective-permute-start.3) | collective-permute-done | bytes 180256 | tf_op jit(solution)/shard_map/ppermute | solution.py:16
  46.3 3.0 collective-permute-start.11
  49.3 3.0 collective-permute-done.4
  53.0 3.0 collective-permute-start.12
  56.0 2.5 collective-permute-done.5
  58.6 2.4 copy.87
  60.9 2.5 convolution_multiply_fusion
  63.5 37.3 %all-gather.5.cloned.1.call-done = bf16[2,1024,576]{2,0,1:T(2,128)(2,1)} async-done(((bf16[2,64,576]{2,0,1:T(2,128)(2,1)}), bf16[2,1024,576]{2,0,1:T(2,128)(2,1)}) %all-gather.5.cloned.1.call-update) | async-done | bytes 2359312 | tf_op jit(solution)/shard_map/all_gather | solution.py:79
  101.4 17.3 %conditional.1 = (f32[64,8,512]{2,1,0:T(8,128)}, f32[64,8]{1,0:T(8,128)S(1)}) conditional(s32[]{:T(128)} %convert_element_type.64, (s32[64]{0:T(128)S(1)}, s32[64,2]{1,0:T(8,128)}, pred[64,1024]{1,0:T(8,128)(4,1)}, bf16[64,8,576]{2,1,0:T(8,128)(2,1)}, bf16[2,1024,576]{2,0,1:T(2,128)(2,1)}, /*index=5*/f32[64,8,1024]{2,1,0:T(8,128)S(1)}, ...), branch_computations={%region_5.8_spmd, %region_8.11_spmd} | conditional | flops 2843409920 | bytes 58866812 | solution.py:129
  101.4 7.3 %copy.90 = bf16[2,1024,576]{1,2,0:T(8,128)(2,1)} copy(bf16[2,1024,576]{2,0,1:T(2,128)(2,1)} %get-tuple-element.115) | data formatting | bytes 4718592 | tf_op jit(solution)/shard_map
  110.4 1.7 slice.21
  116.0 2.6 fusion.19
  120.5 69.0 %all-gather.9.cloned.1.call-done = bf16[1024,2048]{0,1:T(8,128)(2,1)} async-done(((bf16[1024,64]{0,1:T(8,128)(2,1)}), bf16[1024,2048]{0,1:T(8,128)(2,1)}) %all-gather.9.cloned.1.call-update) | async-done | bytes 4194320 | tf_op jit(solution)/shard_map/all_gather | solution.py:137
  189.4 3.7 %multiply_reduce_fusion.1 = (f32[64]{0:T(128)S(1)}, f32[64,2048]{1,0:T(8,128)S(1)}) fusion(bf16[1024,2048]{0,1:T(8,128)(2,1)} %all-gather.9.cloned.1.call-done, bf16[8,8,8,128]{3,2,1,0:T(8,128)(2,1)S(1)} %fusion.34, bf16[1,64,2048]{2,1,0:T(8,128)(2,1)} %param.15), kind=kOutput, calls=%fused_computation.61 | convolution fusion | flops 268959680 | bytes 5112064 | tf_op jit(solution)/shard_map/dot_general | solution.py:135
  194.0 2.2 convolution_convert_fusion.1
  196.2 5.9 %all-to-all-start = ((bf16[32,16,2048]{2,1,0:T(8,128)(2,1)}), bf16[32,16,2048]{2,1,0:T(8,128)(2,1)S(1)}, u32[]{:S(2)}, u32[]{:S(2)}) async-start(bf16[32,16,2048]{2,1,0:T(8,128)(2,1)} %bitcast.20), calls=%async_computation | async-start | bytes 4194304 | tf_op jit(solution)/shard_map/all_to_all | solution.py:162
  202.6 5.9 %collective-permute-done.13 = bf16[1,128,704]{1,2,0:T(8,128)(2,1)} collective-permute-done((bf16[1,128,704]{1,2,0:T(8,128)(2,1)}, bf16[1,128,704]{1,2,0:T(8,128)(2,1)}, u32[]{:S(2)}, u32[]{:S(2)}) %collective-permute-start.13) | collective-permute-done | bytes 180256 | tf_op jit(solution)/shard_map/ppermute | solution.py:18
  208.5 3.4 %collective-permute-start.14 = (bf16[1,128,704]{1,2,0:T(8,128)(2,1)}, bf16[1,128,704]{1,2,0:T(8,128)(2,1)S(1)}, u32[]{:S(2)}, u32[]{:S(2)}) collective-permute-start(bf16[1,128,704]{1,2,0:T(8,128)(2,1)} %collective-permute-done.13), channel_id=1, source_target_pairs={{0,480},{32,0},{64,32},{96,64},{128,96},{160,128},{192,160},{224,1... | collective-permute-start | bytes 540680 | tf_op jit(solution)/shard_map/ppermute | solution.py:18
  214.8 1.6 constant_dynamic-update-slice_fusion.30
  216.4 1.7 constant_dynamic-update-slice_fusion.29
  218.1 1.6 constant_dynamic-update-slice_fusion.28
  219.8 1.6 constant_dynamic-update-slice_fusion.27
  221.4 1.6 constant_dynamic-update-slice_fusion.26
  224.7 1.6 constant_dynamic-update-slice_fusion.24
  227.7 1.6 constant_dynamic-update-slice_fusion.21
  229.3 1.6 constant_dynamic-update-slice_fusion.20
  231.0 1.6 constant_dynamic-update-slice_fusion.19
  232.6 1.6 constant_dynamic-update-slice_fusion.18
  234.2 1.6 constant_dynamic-update-slice_fusion.17
  236.6 1.6 constant_dynamic-update-slice_fusion.15
  238.2 1.6 constant_dynamic-update-slice_fusion.14
  239.9 1.7 constant_dynamic-update-slice_fusion.13
  248.0 1.6 constant_dynamic-update-slice_fusion.3
  249.6 1.6 constant_dynamic-update-slice_fusion.2
  253.6 5.7 %fusion.28 = f32[512,1408]{1,0:T(8,128)S(1)} fusion(bf16[512,2048]{1,0:T(8,128)(2,1)S(1)} %bitcast.102, bf16[1,2048,1408]{2,1,0:T(8,128)(2,1)} %all-gather.11.cloned.1.call-done), kind=kOutput, calls=%fused_computation.40 | convolution fusion | flops 2952790016 | bytes 10747904 | tf_op jit(solution)/shard_map/dot_general | solution.py:168
  259.4 5.0 %convolution_convert_fusion = bf16[512,2048]{1,0:T(8,128)(2,1)} fusion(bf16[1,4096,704]{1,2,0:T(8,128)(2,1)} %constant_dynamic-update-slice_fusion, s32[]{:T(128)S(6)} %select_n.52, f32[512,1408]{1,0:T(8,128)S(1)} %fusion.28), kind=kOutput, calls=%fused_computation.43 | convolution fusion | flops 1479606272 | bytes 8126468 | tf_op jit(solution)/shard_map/dot_general | solution.py:173
  264.4 9.9 %all-to-all-start.1 = ((bf16[32,16,2048]{2,1,0:T(8,128)(2,1)}), bf16[32,16,2048]{2,1,0:T(8,128)(2,1)S(1)}, u32[]{:S(2)}, u32[]{:S(2)}) async-start(bf16[32,16,2048]{2,1,0:T(8,128)(2,1)} %bitcast.103), calls=%async_computation.1 | async-start | bytes 4194304 | tf_op jit(solution)/shard_map/all_to_all | solution.py:176
  276.1 46.8 %all-to-all-done.1 = bf16[32,16,2048]{2,1,0:T(8,128)(2,1)S(1)} async-done(((bf16[32,16,2048]{2,1,0:T(8,128)(2,1)}), bf16[32,16,2048]{2,1,0:T(8,128)(2,1)S(1)}, u32[]{:S(2)}, u32[]{:S(2)}) %all-to-all-start.1) | async-done | bytes 2097184 | tf_op jit(solution)/shard_map/all_to_all | solution.py:176
  322.9 3.1 gather_fusion
  326.0 3.9 %reshape.155 = f32[64,6,2048]{2,1,0:T(8,128)} reshape(bf16[384,2048]{1,0:T(8,128)(2,1)} %gather_fusion) | data formatting | bytes 4718592 | tf_op jit(solution)/shard_map/convert_element_type | solution.py:185
  330.0 3.7 %multiply_reduce_fusion = f32[64,2048]{1,0:T(8,128)S(1)} fusion(f32[64,6,2048]{2,1,0:T(8,128)} %reshape.155, f32[64,6]{1,0:T(8,128)S(1)} %copy.96), kind=kLoop, calls=%fused_computation.42 | loop fusion | flops 1441792 | bytes 3671552 | tf_op jit(solution)/shard_map/reduce_sum | solution.py:185
  (141 shorter events, 35.6 us)
Async XLA Ops:
  6.5 113.5 %copy-start = (bf16[8,512,128]{2,1,0:T(8,128)(2,1)S(1)}, bf16[8,512,128]{2,1,0:T(8,128)(2,1)}, u32[]{:S(2)}) copy-start(bf16[8,512,128]{2,1,0:T(8,128)(2,1)} %param.21) | copy-start | bytes 3145732
  6.5 52.0 %all-gather.7.cloned.1.call-start = ((), (), s32[]{:S(2)}) async-start(), calls=%async_computation.3 | async-start | bytes 1392640 | tf_op jit(solution)/shard_map/all_gather | solution.py:78
  7.3 93.5 %all-gather.5.cloned.1.call-start = ((), (), s32[]{:S(2)}) async-start(), calls=%async_computation.2 | async-start | bytes 2785280 | tf_op jit(solution)/shard_map/all_gather | solution.py:79
  9.1 180.3 %all-gather.9.cloned.1.call-start = ((), (), s32[]{:S(2)}) async-start(), calls=%async_computation.4 | async-start | bytes 4325376 | tf_op jit(solution)/shard_map/all_gather | solution.py:137
  9.8 243.8 %all-gather.11.cloned.1.call-start = ((), (), s32[]{:S(2)}) async-start(), calls=%async_computation.5 | async-start | bytes 6127616 | tf_op jit(solution)/shard_map/all_gather | solution.py:164
  10.4 14.9 %collective-permute-start = (bf16[1,128,704]{1,2,0:T(8,128)(2,1)}, bf16[1,128,704]{1,2,0:T(8,128)(2,1)S(1)}, u32[]{:S(2)}, u32[]{:S(2)}) collective-permute-start(bf16[1,128,704]{1,2,0:T(8,128)(2,1)} %param.27), channel_id=1, source_target_pairs={{0,32},{32,64},{64,96},{96,128},{128,160},{160,192},{192,224},{224... | collective-permute-start | bytes 540680 | tf_op jit(solution)/shard_map/ppermute | solution.py:16
  10.4 21.5 %collective-permute-start.8 = (bf16[1,128,704]{1,2,0:T(8,128)(2,1)}, bf16[1,128,704]{1,2,0:T(8,128)(2,1)S(1)}, u32[]{:S(2)}, u32[]{:S(2)}) collective-permute-start(bf16[1,128,704]{1,2,0:T(8,128)(2,1)} %param.27), channel_id=1, source_target_pairs={{0,480},{32,0},{64,32},{96,64},{128,96},{160,128},{192,160},{224,1... | collective-permute-start | bytes 540680 | tf_op jit(solution)/shard_map/ppermute | solution.py:18
  25.3 76.0 %copy-start.8 = (bf16[1,128,704]{1,2,0:T(8,128)(2,1)}, bf16[1,128,704]{1,2,0:T(8,128)(2,1)S(1)}, u32[]{:S(2)}) copy-start(bf16[1,128,704]{1,2,0:T(8,128)(2,1)S(1)} %collective-permute-done) | copy-start | bytes 540676
  25.3 6.1 %collective-permute-start.1 = (bf16[1,128,704]{1,2,0:T(8,128)(2,1)S(1)}, bf16[1,128,704]{1,2,0:T(8,128)(2,1)S(1)}, u32[]{:S(2)}, u32[]{:S(2)}) collective-permute-start(bf16[1,128,704]{1,2,0:T(8,128)(2,1)S(1)} %collective-permute-done), channel_id=1, source_target_pairs={{0,32},{32,64},{64,96},{96,128},{128,160},{160,192},{192,224},{224... | collective-permute-start | bytes 540680 | tf_op jit(solution)/shard_map/ppermute | solution.py:16
  31.5 27.0 %copy-start.10 = (bf16[1,128,704]{1,2,0:T(8,128)(2,1)}, bf16[1,128,704]{1,2,0:T(8,128)(2,1)S(1)}, u32[]{:S(2)}) copy-start(bf16[1,128,704]{1,2,0:T(8,128)(2,1)S(1)} %collective-permute-done.1) | copy-start | bytes 540676
  31.5 7.0 %collective-permute-start.2 = (bf16[1,128,704]{1,2,0:T(8,128)(2,1)S(1)}, bf16[1,128,704]{1,2,0:T(8,128)(2,1)S(1)}, u32[]{:S(2)}, u32[]{:S(2)}) collective-permute-start(bf16[1,128,704]{1,2,0:T(8,128)(2,1)S(1)} %collective-permute-done.1), channel_id=1, source_target_pairs={{0,32},{32,64},{64,96},{96,128},{128,160},{160,192},{192,224},{224... | collective-permute-start | bytes 540680 | tf_op jit(solution)/shard_map/ppermute | solution.py:16
  32.0 6.6 %collective-permute-start.9 = (bf16[1,128,704]{1,2,0:T(8,128)(2,1)S(1)}, bf16[1,128,704]{1,2,0:T(8,128)(2,1)S(1)}, u32[]{:S(2)}, u32[]{:S(2)}) collective-permute-start(bf16[1,128,704]{1,2,0:T(8,128)(2,1)S(1)} %collective-permute-done.8), channel_id=1, source_target_pairs={{0,480},{32,0},{64,32},{96,64},{128,96},{160,128},{192,160},{224,1... | collective-permute-start | bytes 540680 | tf_op jit(solution)/shard_map/ppermute | solution.py:18
  38.5 20.1 %copy-start.12 = (bf16[1,128,704]{1,2,0:T(8,128)(2,1)}, bf16[1,128,704]{1,2,0:T(8,128)(2,1)S(1)}, u32[]{:S(2)}) copy-start(bf16[1,128,704]{1,2,0:T(8,128)(2,1)S(1)} %collective-permute-done.2) | copy-start | bytes 540676
  38.5 7.0 %collective-permute-start.3 = (bf16[1,128,704]{1,2,0:T(8,128)(2,1)S(1)}, bf16[1,128,704]{1,2,0:T(8,128)(2,1)S(1)}, u32[]{:S(2)}, u32[]{:S(2)}) collective-permute-start(bf16[1,128,704]{1,2,0:T(8,128)(2,1)S(1)} %collective-permute-done.2), channel_id=1, source_target_pairs={{0,32},{32,64},{64,96},{96,128},{128,160},{160,192},{192,224},{224... | collective-permute-start | bytes 540680 | tf_op jit(solution)/shard_map/ppermute | solution.py:16
  38.5 20.0 %copy-start.14 = (bf16[1,128,704]{1,2,0:T(8,128)(2,1)}, bf16[1,128,704]{1,2,0:T(8,128)(2,1)S(1)}, u32[]{:S(2)}) copy-start(bf16[1,128,704]{1,2,0:T(8,128)(2,1)S(1)} %collective-permute-done.9) | copy-start | bytes 540676
  38.5 7.8 %collective-permute-start.10 = (bf16[1,128,704]{1,2,0:T(8,128)(2,1)S(1)}, bf16[1,128,704]{1,2,0:T(8,128)(2,1)S(1)}, u32[]{:S(2)}, u32[]{:S(2)}) collective-permute-start(bf16[1,128,704]{1,2,0:T(8,128)(2,1)S(1)} %collective-permute-done.9), channel_id=1, source_target_pairs={{0,480},{32,0},{64,32},{96,64},{128,96},{160,128},{192,160},{224,1... | collective-permute-start | bytes 540680 | tf_op jit(solution)/shard_map/ppermute | solution.py:18
  45.5 13.1 %copy-start.18 = (bf16[1,128,704]{1,2,0:T(8,128)(2,1)}, bf16[1,128,704]{1,2,0:T(8,128)(2,1)S(1)}, u32[]{:S(2)}) copy-start(bf16[1,128,704]{1,2,0:T(8,128)(2,1)S(1)} %collective-permute-done.3) | copy-start | bytes 540676
  45.5 6.8 %collective-permute-start.4 = (bf16[1,128,704]{1,2,0:T(8,128)(2,1)S(1)}, bf16[1,128,704]{1,2,0:T(8,128)(2,1)S(1)}, u32[]{:S(2)}, u32[]{:S(2)}) collective-permute-start(bf16[1,128,704]{1,2,0:T(8,128)(2,1)S(1)} %collective-permute-done.3), channel_id=1, source_target_pairs={{0,32},{32,64},{64,96},{96,128},{128,160},{160,192},{192,224},{224... | collective-permute-start | bytes 540680 | tf_op jit(solution)/shard_map/ppermute | solution.py:16
  46.3 12.2 %copy-start.16 = (bf16[1,128,704]{1,2,0:T(8,128)(2,1)}, bf16[1,128,704]{1,2,0:T(8,128)(2,1)S(1)}, u32[]{:S(2)}) copy-start(bf16[1,128,704]{1,2,0:T(8,128)(2,1)S(1)} %collective-permute-done.10) | copy-start | bytes 540676
  46.3 6.7 %collective-permute-start.11 = (bf16[1,128,704]{1,2,0:T(8,128)(2,1)S(1)}, bf16[1,128,704]{1,2,0:T(8,128)(2,1)}, u32[]{:S(2)}, u32[]{:S(2)}) collective-permute-start(bf16[1,128,704]{1,2,0:T(8,128)(2,1)S(1)} %collective-permute-done.10), channel_id=1, source_target_pairs={{0,480},{32,0},{64,32},{96,64},{128,96},{160,128},{192,160},{224,1... | collective-permute-start | bytes 540680 | tf_op jit(solution)/shard_map/ppermute | solution.py:18
  52.3 6.3 %copy-start.20 = (bf16[1,128,704]{1,2,0:T(8,128)(2,1)}, bf16[1,128,704]{1,2,0:T(8,128)(2,1)S(1)}, u32[]{:S(2)}) copy-start(bf16[1,128,704]{1,2,0:T(8,128)(2,1)S(1)} %collective-permute-done.4) | copy-start | bytes 540676
  52.3 6.2 %collective-permute-start.5 = (bf16[1,128,704]{1,2,0:T(8,128)(2,1)S(1)}, bf16[1,128,704]{1,2,0:T(8,128)(2,1)}, u32[]{:S(2)}, u32[]{:S(2)}) collective-permute-start(bf16[1,128,704]{1,2,0:T(8,128)(2,1)S(1)} %collective-permute-done.4), channel_id=1, source_target_pairs={{0,32},{32,64},{64,96},{96,128},{128,160},{160,192},{192,224},{224... | collective-permute-start | bytes 540680 | tf_op jit(solution)/shard_map/ppermute | solution.py:16
  53.0 149.0 %collective-permute-start.12 = (bf16[1,128,704]{1,2,0:T(8,128)(2,1)}, bf16[1,128,704]{1,2,0:T(8,128)(2,1)}, u32[]{:S(2)}, u32[]{:S(2)}) collective-permute-start(bf16[1,128,704]{1,2,0:T(8,128)(2,1)} %collective-permute-done.11), channel_id=1, source_target_pairs={{0,480},{32,0},{64,32},{96,64},{128,96},{160,128},{192,160},{224,1... | collective-permute-start | bytes 540680 | tf_op jit(solution)/shard_map/ppermute | solution.py:18
  58.5 143.6 %collective-permute-start.6 = (bf16[1,128,704]{1,2,0:T(8,128)(2,1)}, bf16[1,128,704]{1,2,0:T(8,128)(2,1)}, u32[]{:S(2)}, u32[]{:S(2)}) collective-permute-start(bf16[1,128,704]{1,2,0:T(8,128)(2,1)} %collective-permute-done.5), channel_id=1, source_target_pairs={{0,32},{32,64},{64,96},{96,128},{128,160},{160,192},{192,224},{224... | collective-permute-start | bytes 540680 | tf_op jit(solution)/shard_map/ppermute | solution.py:16
  108.8 3.3 copy-start.3
  108.8 3.3 copy-start.5
  110.3 4.0 %copy-start.4 = (bf16[1024,576]{0,1:T(8,128)(2,1)}, bf16[1024,576]{0,1:T(8,128)(2,1)S(1)}, u32[]{:S(2)}) copy-start(bf16[1024,576]{0,1:T(8,128)(2,1)S(1)} %dynamic-slice_bitcast_fusion) | copy-start | bytes 3538948 | tf_op jit(solution)/shard_map/cond
  110.4 4.0 %copy-start.23 = (pred[64,1024]{1,0:T(8,128)(4,1)S(1)}, pred[64,1024]{1,0:T(8,128)(4,1)}, u32[]{:S(2)}) copy-start(pred[64,1024]{1,0:T(8,128)(4,1)} %get-tuple-element.40) | copy-start | bytes 196612 | tf_op jit(solution)/shard_map/cond
  114.4 1.6 slice-start.1
  118.7 75.3 %copy-start.24 = (s32[512,64]{0,1:T(8,128)S(1)}, s32[512,64]{0,1:T(8,128)}, u32[]{:S(2)}) copy-start(s32[512,64]{0,1:T(8,128)} %convert_reduce_fusion) | copy-start | bytes 393220
  118.7 75.3 %copy-start.27 = (f32[2048]{0:T(1024)S(1)}, f32[2048]{0:T(1024)}, u32[]{:S(2)}) copy-start(f32[2048]{0:T(1024)} %param.23) | copy-start | bytes 24580
  193.1 0.8 copy-start.1
  193.1 33.1 %copy-start.7 = (bf16[1,128,704]{1,2,0:T(8,128)(2,1)S(1)}, bf16[1,128,704]{1,2,0:T(8,128)(2,1)}, u32[]{:S(2)}) copy-start(bf16[1,128,704]{1,2,0:T(8,128)(2,1)} %param.27) | copy-start | bytes 540676
  196.2 57.4 %all-to-all-start = ((bf16[32,16,2048]{2,1,0:T(8,128)(2,1)}), bf16[32,16,2048]{2,1,0:T(8,128)(2,1)S(1)}, u32[]{:S(2)}, u32[]{:S(2)}) async-start(bf16[32,16,2048]{2,1,0:T(8,128)(2,1)} %bitcast.20), calls=%async_computation | async-start | bytes 4194304 | tf_op jit(solution)/shard_map/all_to_all | solution.py:162
  202.0 6.5 %collective-permute-start.13 = (bf16[1,128,704]{1,2,0:T(8,128)(2,1)}, bf16[1,128,704]{1,2,0:T(8,128)(2,1)}, u32[]{:S(2)}, u32[]{:S(2)}) collective-permute-start(bf16[1,128,704]{1,2,0:T(8,128)(2,1)} %collective-permute-done.12), channel_id=1, source_target_pairs={{0,480},{32,0},{64,32},{96,64},{128,96},{160,128},{192,160},{224,1... | collective-permute-start | bytes 540680 | tf_op jit(solution)/shard_map/ppermute | solution.py:18
  202.1 11.1 %collective-permute-start.7 = (bf16[1,128,704]{1,2,0:T(8,128)(2,1)}, bf16[1,128,704]{1,2,0:T(8,128)(2,1)}, u32[]{:S(2)}, u32[]{:S(2)}) collective-permute-start(bf16[1,128,704]{1,2,0:T(8,128)(2,1)} %collective-permute-done.6), channel_id=1, source_target_pairs={{0,32},{32,64},{64,96},{96,128},{128,160},{160,192},{192,224},{224... | collective-permute-start | bytes 540680 | tf_op jit(solution)/shard_map/ppermute | solution.py:16
  202.6 39.0 %copy-start.21 = (bf16[1,128,704]{1,2,0:T(8,128)(2,1)S(1)}, bf16[1,128,704]{1,2,0:T(8,128)(2,1)}, u32[]{:S(2)}) copy-start(bf16[1,128,704]{1,2,0:T(8,128)(2,1)} %copy-done.20) | copy-start | bytes 540676
  202.6 39.7 %copy-start.19 = (bf16[1,128,704]{1,2,0:T(8,128)(2,1)S(1)}, bf16[1,128,704]{1,2,0:T(8,128)(2,1)}, u32[]{:S(2)}) copy-start(bf16[1,128,704]{1,2,0:T(8,128)(2,1)} %copy-done.18) | copy-start | bytes 540676
  202.6 40.4 %copy-start.13 = (bf16[1,128,704]{1,2,0:T(8,128)(2,1)S(1)}, bf16[1,128,704]{1,2,0:T(8,128)(2,1)}, u32[]{:S(2)}) copy-start(bf16[1,128,704]{1,2,0:T(8,128)(2,1)} %copy-done.12) | copy-start | bytes 540676
  202.6 41.1 %copy-start.11 = (bf16[1,128,704]{1,2,0:T(8,128)(2,1)S(1)}, bf16[1,128,704]{1,2,0:T(8,128)(2,1)}, u32[]{:S(2)}) copy-start(bf16[1,128,704]{1,2,0:T(8,128)(2,1)} %copy-done.10) | copy-start | bytes 540676
  202.6 41.8 %copy-start.9 = (bf16[1,128,704]{1,2,0:T(8,128)(2,1)S(1)}, bf16[1,128,704]{1,2,0:T(8,128)(2,1)}, u32[]{:S(2)}) copy-start(bf16[1,128,704]{1,2,0:T(8,128)(2,1)} %copy-done.8) | copy-start | bytes 540676
  202.6 44.0 %copy-start.15 = (bf16[1,128,704]{1,2,0:T(8,128)(2,1)S(1)}, bf16[1,128,704]{1,2,0:T(8,128)(2,1)}, u32[]{:S(2)}) copy-start(bf16[1,128,704]{1,2,0:T(8,128)(2,1)} %copy-done.14) | copy-start | bytes 540676
  202.6 44.7 %copy-start.17 = (bf16[1,128,704]{1,2,0:T(8,128)(2,1)S(1)}, bf16[1,128,704]{1,2,0:T(8,128)(2,1)}, u32[]{:S(2)}) copy-start(bf16[1,128,704]{1,2,0:T(8,128)(2,1)} %copy-done.16) | copy-start | bytes 540676
  208.5 27.3 %collective-permute-start.14 = (bf16[1,128,704]{1,2,0:T(8,128)(2,1)}, bf16[1,128,704]{1,2,0:T(8,128)(2,1)S(1)}, u32[]{:S(2)}, u32[]{:S(2)}) collective-permute-start(bf16[1,128,704]{1,2,0:T(8,128)(2,1)} %collective-permute-done.13), channel_id=1, source_target_pairs={{0,480},{32,0},{64,32},{96,64},{128,96},{160,128},{192,160},{224,1... | collective-permute-start | bytes 540680 | tf_op jit(solution)/shard_map/ppermute | solution.py:18
  259.3 15.1 %copy-start.28 = (s32[1,64,6]{1,0,2:T(1,128)S(1)}, s32[1,64,6]{1,0,2:T(1,128)}, u32[]{:S(2)}) copy-start(s32[1,64,6]{1,0,2:T(1,128)} %param.25) | copy-start | bytes 4612
  259.3 15.2 %copy-start.26 = (bf16[2048,32]{0,1:T(8,128)(2,1)S(1)}, bf16[2048,32]{0,1:T(8,128)(2,1)}, u32[]{:S(2)}) copy-start(bf16[2048,32]{0,1:T(8,128)(2,1)} %param.24) | copy-start | bytes 393220
  264.4 58.5 %all-to-all-start.1 = ((bf16[32,16,2048]{2,1,0:T(8,128)(2,1)}), bf16[32,16,2048]{2,1,0:T(8,128)(2,1)S(1)}, u32[]{:S(2)}, u32[]{:S(2)}) async-start(bf16[32,16,2048]{2,1,0:T(8,128)(2,1)} %bitcast.103), calls=%async_computation.1 | async-start | bytes 4194304 | tf_op jit(solution)/shard_map/all_to_all | solution.py:176
  326.0 7.7 %copy-start.2 = (f32[64,2048]{1,0:T(8,128)S(1)}, f32[64,2048]{1,0:T(8,128)}, u32[]{:S(2)}) copy-start(f32[64,2048]{1,0:T(8,128)} %copy-done.1) | copy-start | bytes 1572868
Sparse Core Ops, SparseCore 0:
  9.5 46.7 all-gather.6
  58.4 42.2 all-gather.4
  103.9 85.4 all-gather.8
  191.4 48.3 all-gather.10
